TPU v7x, 512 devices: a whole 4x4x16 slice. The times are simulated.
512 devices in a mesh: sub: 128 (over y, z, core), case: 4 (over x).
Axes of the slice: x: 4, y: 4, z: 16, core: 2. Of those that a mesh axis runs over, the one named last changes fastest.
Arguments:
- load_interior: float32 [128, 128, 4096], P('sub', None, 'case'), may hold values from -6 to 6
- load_boundary: float32 [128, 128, 1024], P('sub', None, 'case'), may hold values from -6 to 6
- cond_blocks: float32 [128, 128, 4096], P('sub', 'case'), may hold values from -0.25 to 0.25
- block_rows: int32 [128, 128], P('sub', 'case'), may hold values from 0 to 15
- block_cols: int32 [128, 128], P('sub', 'case'), may hold values from 0 to 63, as said below
- interface_maps: int32 [128, 7, 2, 1024], P('sub'), may hold values from 0 to 1023, as said below
- merge_maps: float32 [128, 7, 1024, 512], P('sub', None, 'case'), as said below
Outputs:
- leaf_loads: float32 [128, 1024, 128], P('sub', 'case')
- node_loads: float32 [128, 1024, 128], P('sub', 'case')
Inputs may be any that keep to these rules, and one draw needn't show every extreme that they name: `block_cols`: entry k of a substructure's row lies in [(k // 32) * 16, (k // 32 + 1) * 16); blocks may repeat. `interface_maps`: each row of 1024 entries is a permutation; at level index l, slots that agree in all but their lowest l + 1 bits hold equal entries. `merge_maps`: at level index l, slots that agree in all but their lowest l + 1 bits hold equal entries.
All inputs are finite; a program needn't handle non-finite values.
Results may differ from a plain program's by a relative error of at most 0.0003.
Values sent between devices are 32-bit elements; how exact they have to be, the bound alone decides.
No kernel may reach another device: no remote copies, remote signals or barrier semaphores. Data moves between devices by JAX's collectives and lax.ppermute only.
A program may use at most 64 MiB of HBM per device.

v0:
```python
import jax
import jax.numpy as jnp
from jax import lax
from jax.sharding import PartitionSpec as P

BLK = 64


def from_partner(value, axis, distance):
    mask = 2**distance
    pairs = [(source, source ^ mask) for source in range(lax.axis_size(axis))]
    return lax.ppermute(value, axis, pairs)


def on_device(
    load_interior, load_boundary, cond_blocks, block_rows, block_cols, interface_maps, merge_maps
):
    interior, boundary = (
        lax.all_to_all(load_interior, "sub", split_axis=1, concat_axis=0, tiled=True),
        lax.all_to_all(load_boundary, "sub", split_axis=1, concat_axis=0, tiled=True),
    )
    interior = jnp.transpose(interior[:, 0, :])
    boundary = jnp.transpose(boundary[:, 0, :])
    local_rows = interior.shape[0]
    num_cases = interior.shape[1]
    block_count = cond_blocks.shape[1]
    block_size = BLK
    blocks = cond_blocks[0].reshape(block_count, block_size, block_size)
    quarter = boundary.shape[0]
    groups = lax.axis_size("case")
    full_rows = quarter * groups
    position = lax.axis_index("case")
    local_cols = block_cols[0] - position * (local_rows // block_size)
    pieces = jnp.take(
        interior.reshape(local_rows // block_size, block_size, num_cases), local_cols, axis=0
    )
    products = jnp.einsum("krc,kcn->krn", blocks, pieces, precision=lax.Precision.HIGHEST)
    row_blocks = full_rows // block_size
    onehot = (block_rows[0][None, :] == jnp.arange(row_blocks, dtype=jnp.int32)[:, None]).astype(
        jnp.float32
    )
    partial_value = jnp.dot(
        onehot,
        products.reshape(block_count, block_size * num_cases),
        precision=lax.Precision.HIGHEST,
    )
    partial_value = partial_value.reshape(full_rows, num_cases)
    embedded = lax.dynamic_update_slice(
        jnp.zeros((full_rows, num_cases), jnp.float32), boundary, (position * quarter, 0)
    )
    contribution = embedded - partial_value
    current = lax.psum(contribution, "case")
    leaf_share = lax.dynamic_slice_in_dim(current, position * quarter, quarter, 0)
    slot = lax.axis_index("sub")
    levels = lax.axis_size("sub").bit_length() - 1
    nodes = jnp.zeros((quarter, num_cases), jnp.float32)
    for level in range(1, levels + 1):
        half = 1 << level - 1
        maps = interface_maps[0, level - 1]
        matrix = merge_maps[0, level - 1]
        shared_rows = matrix.shape[1]
        kept_index = jnp.concatenate([maps[0, shared_rows:], maps[1, shared_rows:] + full_rows])
        mine = lax.dynamic_slice_in_dim(kept_index, position * quarter, quarter)
        other = from_partner(current, "sub", level - 1)
        own_full, other_full = (current, other)
        upper = slot // half % 2 == 1
        left_full = jnp.where(upper, other_full, own_full)
        right_full = jnp.where(upper, own_full, other_full)
        stacked = jnp.concatenate([left_full, right_full], axis=0)
        shared = jnp.take(stacked, maps[0, :shared_rows], axis=0) + jnp.take(
            stacked, maps[1, :shared_rows] + full_rows, axis=0
        )
        parent = jnp.take(stacked, mine, axis=0) - jnp.dot(
            matrix, shared, precision=lax.Precision.HIGHEST
        )
        is_node = slot % (2 * half) == half
        if level == levels:
            is_node = jnp.logical_or(is_node, slot == 0)
        nodes = jnp.where(is_node, parent, nodes)
        if level < levels:
            current = lax.all_gather(parent, "case", axis=0, tiled=True)
    return (leaf_share[None], nodes[None])


def solution(mesh):
    placed = (
        P("sub", None, "case"),
        P("sub", None, "case"),
        P("sub", "case", None),
        P("sub", "case"),
        P("sub", "case"),
        P("sub", None, None, None),
        P("sub", None, "case", None),
    )
    return jax.shard_map(
        on_device,
        mesh=mesh,
        in_specs=placed,
        out_specs=(P("sub", "case", None), P("sub", "case", None)),
        check_vma=False,
    )
```

profile of v0, /device:TPU:8, one launch (start us, length us, event | category | flops | bytes accessed | tf_op | source)
XLA Modules:
  0.0 423.4 jit_solution(13161478264808261519)
XLA Ops:
  7.2 1.7 copy.64
  8.9 19.6 %all-to-all-start = ((f32[1,128,256]{2,0,1:T(1,128)}), f32[1,128,256]{2,0,1:T(1,128)S(1)}, u32[]{:S(2)}, u32[]{:S(2)}) async-start(f32[1,128,256]{2,0,1:T(1,128)} %copy.64), calls=%async_computation | async-start | bytes 262144 | tf_op jit(solution)/shard_map/all_to_all | solution.py:20
  28.5 2.4 copy.66
  30.9 0.7 fusion.59
  31.5 0.8 slice_bitcast_fusion
  32.8 12.9 %all-to-all-done = f32[1,128,256]{2,0,1:T(1,128)S(1)} async-done(((f32[1,128,256]{2,0,1:T(1,128)}), f32[1,128,256]{2,0,1:T(1,128)S(1)}, u32[]{:S(2)}, u32[]{:S(2)}) %all-to-all-start) | async-done | bytes 131104 | tf_op jit(solution)/shard_map/all_to_all | solution.py:20
  45.7 7.2 %all-to-all-start.1 = ((f32[1,128,1024]{2,0,1:T(1,128)}), f32[1,128,1024]{2,0,1:T(1,128)S(1)}, u32[]{:S(2)}, u32[]{:S(2)}) async-start(f32[1,128,1024]{2,0,1:T(1,128)} %copy.66), calls=%async_computation.1 | async-start | bytes 1048576 | tf_op jit(solution)/shard_map/all_to_all | solution.py:19
  53.2 1.5 reshape_squeeze.3
  55.1 31.4 %all-to-all-done.1 = f32[1,128,1024]{2,0,1:T(1,128)S(1)} async-done(((f32[1,128,1024]{2,0,1:T(1,128)}), f32[1,128,1024]{2,0,1:T(1,128)S(1)}, u32[]{:S(2)}, u32[]{:S(2)}) %all-to-all-start.1) | async-done | bytes 524320 | tf_op jit(solution)/shard_map/all_to_all | solution.py:19
  87.6 1.2 fusion.12
  88.8 1.1 fusion.9
  89.9 0.9 sub.69
  90.9 50.0 %all-reduce.2.cloned.1.call-done = f32[1024,128]{1,0:T(8,128)} async-done(((f32[1024,128]{1,0:T(8,128)}), f32[1024,128]{1,0:T(8,128)}) %all-reduce.2.cloned.1.call-update) | async-done | bytes 524304 | tf_op jit(solution)/shard_map/psum | solution.py:52
  140.8 1.9 collective-permute-start
  142.8 2.0 collective-permute-done
  144.9 1.1 broadcast_select_fusion.1
  146.0 1.0 gather_fusion.3
  147.1 1.0 gather_fusion.2
  148.1 0.7 gather_fusion.1
  149.0 1.9 fusion.8
  150.9 12.8 %all_gather.18 = f32[1024,128]{0,1:T(8,128)S(1)} all-gather(f32[256,128]{0,1:T(8,128)S(1)} %fusion.8), channel_id=1, replica_groups=mesh['sub'=128,'case'=4] {'case'}, dimensions={0}, use_global_device_ids=true | all-gather | bytes 655360 | tf_op jit(solution)/shard_map/all_gather | solution.py:81
  163.6 3.6 collective-permute-start.1
  167.4 9.3 %collective-permute-done.1 = f32[1024,128]{0,1:T(8,128)S(1)} collective-permute-done((f32[1024,128]{0,1:T(8,128)S(1)}, f32[1024,128]{0,1:T(8,128)S(1)}, u32[]{:S(2)}, u32[]{:S(2)}) %collective-permute-start.1) | collective-permute-done | bytes 524320 | tf_op jit(solution)/shard_map/ppermute | solution.py:12
  177.2 1.0 gather_fusion.6
  178.2 1.0 gather_fusion.5
  179.3 0.7 gather_fusion.4
  180.1 1.9 fusion.7
  182.0 13.1 %all_gather.19 = f32[1024,128]{0,1:T(8,128)S(1)} all-gather(f32[256,128]{0,1:T(8,128)S(1)} %fusion.7), channel_id=1, replica_groups=mesh['sub'=128,'case'=4] {'case'}, dimensions={0}, use_global_device_ids=true | all-gather | bytes 655360 | tf_op jit(solution)/shard_map/all_gather | solution.py:81
  195.1 4.4 %collective-permute-start.2 = (f32[1024,128]{0,1:T(8,128)S(1)}, f32[1024,128]{0,1:T(8,128)S(1)}, u32[]{:S(2)}, u32[]{:S(2)}) collective-permute-start(f32[1024,128]{0,1:T(8,128)S(1)} %all_gather.19), channel_id=1, source_target_pairs={{0,16},{4,20},{8,24},{12,28},{16,0},{20,4},{24,8},{28,12},{32,48},... | collective-permute-start | bytes 1572872 | tf_op jit(solution)/shard_map/ppermute | solution.py:12
  199.6 16.8 %collective-permute-done.2 = f32[1024,128]{0,1:T(8,128)S(1)} collective-permute-done((f32[1024,128]{0,1:T(8,128)S(1)}, f32[1024,128]{0,1:T(8,128)S(1)}, u32[]{:S(2)}, u32[]{:S(2)}) %collective-permute-start.2) | collective-permute-done | bytes 524320 | tf_op jit(solution)/shard_map/ppermute | solution.py:12
  217.0 1.0 gather_fusion.9
  218.0 1.0 gather_fusion.8
  219.1 0.7 gather_fusion.7
  219.9 1.9 fusion.6
  221.8 13.3 %all_gather.20 = f32[1024,128]{0,1:T(8,128)S(1)} all-gather(f32[256,128]{0,1:T(8,128)S(1)} %fusion.6), channel_id=1, replica_groups=mesh['sub'=128,'case'=4] {'case'}, dimensions={0}, use_global_device_ids=true | all-gather | bytes 655360 | tf_op jit(solution)/shard_map/all_gather | solution.py:81
  235.1 7.6 %collective-permute-start.3 = (f32[1024,128]{0,1:T(8,128)S(1)}, f32[1024,128]{0,1:T(8,128)S(1)}, u32[]{:S(2)}, u32[]{:S(2)}) collective-permute-start(f32[1024,128]{0,1:T(8,128)S(1)} %all_gather.20), channel_id=1, source_target_pairs={{0,32},{4,36},{8,40},{12,44},{16,48},{20,52},{24,56},{28,60},{32,0... | collective-permute-start | bytes 1572872 | tf_op jit(solution)/shard_map/ppermute | solution.py:12
  242.8 40.0 %collective-permute-done.3 = f32[1024,128]{0,1:T(8,128)S(1)} collective-permute-done((f32[1024,128]{0,1:T(8,128)S(1)}, f32[1024,128]{0,1:T(8,128)S(1)}, u32[]{:S(2)}, u32[]{:S(2)}) %collective-permute-start.3) | collective-permute-done | bytes 524320 | tf_op jit(solution)/shard_map/ppermute | solution.py:12
  283.3 1.0 gather_fusion.12
  284.3 1.0 gather_fusion.11
  285.4 0.7 gather_fusion.10
  286.2 1.9 fusion.5
  288.1 12.8 %all_gather.21 = f32[1024,128]{0,1:T(8,128)S(1)} all-gather(f32[256,128]{0,1:T(8,128)S(1)} %fusion.5), channel_id=1, replica_groups=mesh['sub'=128,'case'=4] {'case'}, dimensions={0}, use_global_device_ids=true | all-gather | bytes 655360 | tf_op jit(solution)/shard_map/all_gather | solution.py:81
  300.9 11.2 %collective-permute-start.4 = (f32[1024,128]{0,1:T(8,128)S(1)}, f32[1024,128]{0,1:T(8,128)S(1)}, u32[]{:S(2)}, u32[]{:S(2)}) collective-permute-start(f32[1024,128]{0,1:T(8,128)S(1)} %all_gather.21), channel_id=1, source_target_pairs={{0,64},{4,68},{8,72},{12,76},{16,80},{20,84},{24,88},{28,92},{32,9... | collective-permute-start | bytes 1572872 | tf_op jit(solution)/shard_map/ppermute | solution.py:12
  312.1 36.2 %collective-permute-done.4 = f32[1024,128]{0,1:T(8,128)S(1)} collective-permute-done((f32[1024,128]{0,1:T(8,128)S(1)}, f32[1024,128]{0,1:T(8,128)S(1)}, u32[]{:S(2)}, u32[]{:S(2)}) %collective-permute-start.4) | collective-permute-done | bytes 524320 | tf_op jit(solution)/shard_map/ppermute | solution.py:12
  348.8 1.0 gather_fusion.15
  349.9 1.0 gather_fusion.14
  350.9 0.7 gather_fusion.13
  351.7 1.9 fusion.4
  353.6 13.2 %all_gather.22 = f32[1024,128]{0,1:T(8,128)S(1)} all-gather(f32[256,128]{0,1:T(8,128)S(1)} %fusion.4), channel_id=1, replica_groups=mesh['sub'=128,'case'=4] {'case'}, dimensions={0}, use_global_device_ids=true | all-gather | bytes 655360 | tf_op jit(solution)/shard_map/all_gather | solution.py:81
  366.8 2.4 collective-permute-start.5
  369.3 10.0 %collective-permute-done.5 = f32[1024,128]{0,1:T(8,128)S(1)} collective-permute-done((f32[1024,128]{0,1:T(8,128)S(1)}, f32[1024,128]{0,1:T(8,128)S(1)}, u32[]{:S(2)}, u32[]{:S(2)}) %collective-permute-start.5) | collective-permute-done | bytes 524320 | tf_op jit(solution)/shard_map/ppermute | solution.py:12
  379.8 1.0 gather_fusion.18
  380.8 1.0 gather_fusion.17
  381.8 0.7 gather_fusion.16
  382.7 1.9 fusion.3
  384.6 13.3 %all_gather.23 = f32[1024,128]{0,1:T(8,128)S(1)} all-gather(f32[256,128]{0,1:T(8,128)S(1)} %fusion.3), channel_id=1, replica_groups=mesh['sub'=128,'case'=4] {'case'}, dimensions={0}, use_global_device_ids=true | all-gather | bytes 655360 | tf_op jit(solution)/shard_map/all_gather | solution.py:81
  397.8 4.0 collective-permute-start.6
  401.9 1.6 dynamic-slice_bitcast_fusion
  403.5 6.9 %collective-permute-done.6 = f32[1024,128]{0,1:T(8,128)S(1)} collective-permute-done((f32[1024,128]{0,1:T(8,128)S(1)}, f32[1024,128]{0,1:T(8,128)S(1)}, u32[]{:S(2)}, u32[]{:S(2)}) %collective-permute-start.6) | collective-permute-done | bytes 524320 | tf_op jit(solution)/shard_map/ppermute | solution.py:12
  410.9 1.0 gather_fusion.21
  412.0 1.0 gather_fusion.20
  413.0 0.7 gather_fusion.19
  413.8 1.9 fusion.2
  415.7 0.8 copy.93
  (100 shorter events, 5.7 us)
Async XLA Ops:
  7.2 47.8 %copy-start.1 = (s32[1,32]{1,0:T(1,128)S(1)}, s32[1,32]{1,0:T(1,128)}, u32[]{:S(2)}) copy-start(s32[1,32]{1,0:T(1,128)} %param.15) | copy-start | bytes 388
  8.9 36.8 %all-to-all-start = ((f32[1,128,256]{2,0,1:T(1,128)}), f32[1,128,256]{2,0,1:T(1,128)S(1)}, u32[]{:S(2)}, u32[]{:S(2)}) async-start(f32[1,128,256]{2,0,1:T(1,128)} %copy.64), calls=%async_computation | async-start | bytes 262144 | tf_op jit(solution)/shard_map/all_to_all | solution.py:20
  45.7 40.8 %all-to-all-start.1 = ((f32[1,128,1024]{2,0,1:T(1,128)}), f32[1,128,1024]{2,0,1:T(1,128)S(1)}, u32[]{:S(2)}, u32[]{:S(2)}) async-start(f32[1,128,1024]{2,0,1:T(1,128)} %copy.66), calls=%async_computation.1 | async-start | bytes 1048576 | tf_op jit(solution)/shard_map/all_to_all | solution.py:19
  52.9 87.9 %all-reduce.2.cloned.1.call-start = ((), (), s32[]{:S(2)}) async-start(), calls=%async_computation.2 | async-start | bytes 1048576 | tf_op jit(solution)/shard_map/psum | solution.py:52
  54.9 33.8 %copy-start = (s32[1,32]{1,0:T(1,128)S(1)}, s32[1,32]{1,0:T(1,128)}, u32[]{:S(2)}) copy-start(s32[1,32]{1,0:T(1,128)} %param.14) | copy-start | bytes 388
  140.8 4.0 collective-permute-start
  163.6 13.0 %collective-permute-start.1 = (f32[1024,128]{0,1:T(8,128)S(1)}, f32[1024,128]{0,1:T(8,128)S(1)}, u32[]{:S(2)}, u32[]{:S(2)}) collective-permute-start(f32[1024,128]{0,1:T(8,128)S(1)} %all_gather.18), channel_id=1, source_target_pairs={{0,8},{4,12},{8,0},{12,4},{16,24},{20,28},{24,16},{28,20},{32,40},... | collective-permute-start | bytes 1572872 | tf_op jit(solution)/shard_map/ppermute | solution.py:12
  195.1 21.3 %collective-permute-start.2 = (f32[1024,128]{0,1:T(8,128)S(1)}, f32[1024,128]{0,1:T(8,128)S(1)}, u32[]{:S(2)}, u32[]{:S(2)}) collective-permute-start(f32[1024,128]{0,1:T(8,128)S(1)} %all_gather.19), channel_id=1, source_target_pairs={{0,16},{4,20},{8,24},{12,28},{16,0},{20,4},{24,8},{28,12},{32,48},... | collective-permute-start | bytes 1572872 | tf_op jit(solution)/shard_map/ppermute | solution.py:12
  235.1 47.6 %collective-permute-start.3 = (f32[1024,128]{0,1:T(8,128)S(1)}, f32[1024,128]{0,1:T(8,128)S(1)}, u32[]{:S(2)}, u32[]{:S(2)}) collective-permute-start(f32[1024,128]{0,1:T(8,128)S(1)} %all_gather.20), channel_id=1, source_target_pairs={{0,32},{4,36},{8,40},{12,44},{16,48},{20,52},{24,56},{28,60},{32,0... | collective-permute-start | bytes 1572872 | tf_op jit(solution)/shard_map/ppermute | solution.py:12
  300.9 47.4 %collective-permute-start.4 = (f32[1024,128]{0,1:T(8,128)S(1)}, f32[1024,128]{0,1:T(8,128)S(1)}, u32[]{:S(2)}, u32[]{:S(2)}) collective-permute-start(f32[1024,128]{0,1:T(8,128)S(1)} %all_gather.21), channel_id=1, source_target_pairs={{0,64},{4,68},{8,72},{12,76},{16,80},{20,84},{24,88},{28,92},{32,9... | collective-permute-start | bytes 1572872 | tf_op jit(solution)/shard_map/ppermute | solution.py:12
  366.8 12.5 %collective-permute-start.5 = (f32[1024,128]{0,1:T(8,128)S(1)}, f32[1024,128]{0,1:T(8,128)S(1)}, u32[]{:S(2)}, u32[]{:S(2)}) collective-permute-start(f32[1024,128]{0,1:T(8,128)S(1)} %all_gather.22), channel_id=1, source_target_pairs={{0,128},{4,132},{8,136},{12,140},{16,144},{20,148},{24,152},{28,15... | collective-permute-start | bytes 1572872 | tf_op jit(solution)/shard_map/ppermute | solution.py:12
  397.8 12.6 %collective-permute-start.6 = (f32[1024,128]{0,1:T(8,128)S(1)}, f32[1024,128]{0,1:T(8,128)S(1)}, u32[]{:S(2)}, u32[]{:S(2)}) collective-permute-start(f32[1024,128]{0,1:T(8,128)S(1)} %all_gather.23), channel_id=1, source_target_pairs={{0,256},{4,260},{8,264},{12,268},{16,272},{20,276},{24,280},{28,28... | collective-permute-start | bytes 1572872 | tf_op jit(solution)/shard_map/ppermute | solution.py:12
Sparse Core Ops, SparseCore 0:
  91.0 49.8 all-reduce.1
where the time goes:
time: 424 us; the launch traced here: 423 us
  waiting for transfers between devices  215 us (51%)
  blocking collectives  78.5 us (19%)
  starting transfers between devices  62.1 us (15%)
  local copies, waits for them, and re-layouts  32.1 us (8%)
  matrix products  15.4 us (4%)
  between operations  15.3 us (4%)
  other arithmetic  4.42 us (1%)
    ppermute x7, waiting for transfers between devices, from_partner(): return lax.ppermute(value, axis, pairs)  121 us
    all_gather x6, blocking collectives, on_device(): current = lax.all_gather(parent, 'case', axis=0, tiled=True)  78.5 us
    psum x1, waiting for transfers between devices, on_device(): current = lax.psum(contribution, 'case')  50 us
    ppermute x7, starting transfers between devices, from_partner(): return lax.ppermute(value, axis, pairs)  35.3 us
    all_to_all x1, waiting for transfers between devices, on_device(): lax.all_to_all(load_interior, 'sub', split_axis=1, concat_axis=0, tiled=T...  31.4 us
    all_to_all x1, starting transfers between devices, on_device(): lax.all_to_all(load_boundary, 'sub', split_axis=1, concat_axis=0, tiled=T...  19.6 us
    dot_general x7, matrix products, on_device(): jnp.dot(matrix, shared, precision=lax.Precision.HIGHEST)  13.2 us
    all_to_all x1, waiting for transfers between devices, on_device(): lax.all_to_all(load_boundary, 'sub', split_axis=1, concat_axis=0, tiled=T...  12.9 us
  transfers between devices with their start and end apart: 10, of which 10 were waited for; matrix products, arithmetic and copies ran while one was open for 2% of the time, Pallas kernels for 0%

commit v1 on v0

--- a/solution.py
+++ b/solution.py
@@ -49,7 +49,8 @@
         jnp.zeros((full_rows, num_cases), jnp.float32), boundary, (position * quarter, 0)
     )
     contribution = embedded - partial_value
-    current = lax.psum(contribution, "case")
+    parts = lax.all_gather(contribution, "case")
+    current = jnp.sum(parts, axis=0)
     leaf_share = lax.dynamic_slice_in_dim(current, position * quarter, quarter, 0)
     slot = lax.axis_index("sub")
     levels = lax.axis_size("sub").bit_length() - 1

time: 424 us -> 406 us (0.958)
  waiting for transfers between devices: 215 us -> 197 us
    psum x1 -> x0, waiting for transfers between devices: 50 us -> none  [on_device(): current = lax.psum(contribution, 'case')]
    all_gather x0 -> x1, waiting for transfers between devices: none -> 29.7 us  [on_device(): parts = lax.all_gather(contribution, 'case')]
where the time goes in v1:
time: 406 us; the launch traced here: 405 us
  waiting for transfers between devices  197 us (49%)
  blocking collectives  79.8 us (20%)
  starting transfers between devices  62 us (15%)
  local copies, waits for them, and re-layouts  31.2 us (8%)
  matrix products  15.4 us (4%)
  between operations  15.3 us (4%)
  other arithmetic  4.47 us (1%)
    ppermute x7, waiting for transfers between devices, from_partner(): return lax.ppermute(value, axis, pairs)  121 us
    all_gather x6, blocking collectives, on_device(): current = lax.all_gather(parent, 'case', axis=0, tiled=True)  79.8 us
    ppermute x7, starting transfers between devices, from_partner(): return lax.ppermute(value, axis, pairs)  35.2 us
    all_to_all x1, waiting for transfers between devices, on_device(): lax.all_to_all(load_interior, 'sub', split_axis=1, concat_axis=0, tiled=T...  31.6 us
    all_gather x1, waiting for transfers between devices, on_device(): parts = lax.all_gather(contribution, 'case')  29.7 us
    all_to_all x1, starting transfers between devices, on_device(): lax.all_to_all(load_boundary, 'sub', split_axis=1, concat_axis=0, tiled=T...  19.6 us
    all_to_all x1, waiting for transfers between devices, on_device(): lax.all_to_all(load_boundary, 'sub', split_axis=1, concat_axis=0, tiled=T...  13.8 us
    dot_general x7, matrix products, on_device(): jnp.dot(matrix, shared, precision=lax.Precision.HIGHEST)  13.2 us
  transfers between devices with their start and end apart: 10, of which 10 were waited for; matrix products, arithmetic and copies ran while one was open for 2% of the time, Pallas kernels for 0%

profile of v1, /device:TPU:8, one launch (start us, length us, event | category | flops | bytes accessed | tf_op | source)
XLA Modules:
  0.0 404.8 jit_solution(2131480566072497121)
XLA Ops:
  7.2 1.7 copy.94
  8.9 19.6 %all-to-all-start = ((f32[1,128,256]{2,0,1:T(1,128)}), f32[1,128,256]{2,0,1:T(1,128)S(1)}, u32[]{:S(2)}, u32[]{:S(2)}) async-start(f32[1,128,256]{2,0,1:T(1,128)} %copy.94), calls=%async_computation | async-start | bytes 262144 | tf_op jit(solution)/shard_map/all_to_all | solution.py:20
  28.5 2.4 copy.96
  30.9 0.8 slice_bitcast_fusion
  31.9 13.8 %all-to-all-done = f32[1,128,256]{2,0,1:T(1,128)S(1)} async-done(((f32[1,128,256]{2,0,1:T(1,128)}), f32[1,128,256]{2,0,1:T(1,128)S(1)}, u32[]{:S(2)}, u32[]{:S(2)}) %all-to-all-start) | async-done | bytes 131104 | tf_op jit(solution)/shard_map/all_to_all | solution.py:20
  45.7 7.2 %all-to-all-start.1 = ((f32[1,128,1024]{2,0,1:T(1,128)}), f32[1,128,1024]{2,0,1:T(1,128)S(1)}, u32[]{:S(2)}, u32[]{:S(2)}) async-start(f32[1,128,1024]{2,0,1:T(1,128)} %copy.96), calls=%async_computation.1 | async-start | bytes 1048576 | tf_op jit(solution)/shard_map/all_to_all | solution.py:19
  53.1 1.5 reshape_squeeze.3
  54.9 31.6 %all-to-all-done.1 = f32[1,128,1024]{2,0,1:T(1,128)S(1)} async-done(((f32[1,128,1024]{2,0,1:T(1,128)}), f32[1,128,1024]{2,0,1:T(1,128)S(1)}, u32[]{:S(2)}, u32[]{:S(2)}) %all-to-all-start.1) | async-done | bytes 524320 | tf_op jit(solution)/shard_map/all_to_all | solution.py:19
  86.9 0.6 gather_fusion
  87.6 1.2 fusion.12
  88.8 1.1 fusion.9
  89.9 0.9 sub.69
  91.3 29.7 %all-gather.3.cloned.1.call-done = f32[4096,128]{1,0:T(8,128)} async-done(((f32[1024,128]{1,0:T(8,128)}), f32[4096,128]{1,0:T(8,128)}) %all-gather.3.cloned.1.call-update) | async-done | bytes 2097168 | tf_op jit(solution)/shard_map/all_gather | solution.py:52
  121.0 1.8 reduce_sum.9
  122.7 1.9 collective-permute-start
  124.7 1.8 collective-permute-done
  126.7 1.0 gather_fusion.3
  127.7 1.0 gather_fusion.2
  128.8 0.7 gather_fusion.1
  129.6 1.9 fusion.8
  131.5 13.5 %all_gather.26 = f32[1024,128]{0,1:T(8,128)S(1)} all-gather(f32[256,128]{0,1:T(8,128)S(1)} %fusion.8), channel_id=1, replica_groups=mesh['sub'=128,'case'=4] {'case'}, dimensions={0}, use_global_device_ids=true | all-gather | bytes 655360 | tf_op jit(solution)/shard_map/all_gather | solution.py:82
  145.0 3.6 collective-permute-start.1
  148.8 8.5 %collective-permute-done.1 = f32[1024,128]{0,1:T(8,128)S(1)} collective-permute-done((f32[1024,128]{0,1:T(8,128)S(1)}, f32[1024,128]{0,1:T(8,128)S(1)}, u32[]{:S(2)}, u32[]{:S(2)}) %collective-permute-start.1) | collective-permute-done | bytes 524320 | tf_op jit(solution)/shard_map/ppermute | solution.py:12
  157.8 1.0 gather_fusion.6
  158.8 1.0 gather_fusion.5
  159.9 0.7 gather_fusion.4
  160.7 1.9 fusion.7
  162.6 13.3 %all_gather.27 = f32[1024,128]{0,1:T(8,128)S(1)} all-gather(f32[256,128]{0,1:T(8,128)S(1)} %fusion.7), channel_id=1, replica_groups=mesh['sub'=128,'case'=4] {'case'}, dimensions={0}, use_global_device_ids=true | all-gather | bytes 655360 | tf_op jit(solution)/shard_map/all_gather | solution.py:82
  175.9 4.4 %collective-permute-start.2 = (f32[1024,128]{0,1:T(8,128)S(1)}, f32[1024,128]{0,1:T(8,128)S(1)}, u32[]{:S(2)}, u32[]{:S(2)}) collective-permute-start(f32[1024,128]{0,1:T(8,128)S(1)} %all_gather.27), channel_id=1, source_target_pairs={{0,16},{4,20},{8,24},{12,28},{16,0},{20,4},{24,8},{28,12},{32,48},... | collective-permute-start | bytes 1572872 | tf_op jit(solution)/shard_map/ppermute | solution.py:12
  180.4 16.8 %collective-permute-done.2 = f32[1024,128]{0,1:T(8,128)S(1)} collective-permute-done((f32[1024,128]{0,1:T(8,128)S(1)}, f32[1024,128]{0,1:T(8,128)S(1)}, u32[]{:S(2)}, u32[]{:S(2)}) %collective-permute-start.2) | collective-permute-done | bytes 524320 | tf_op jit(solution)/shard_map/ppermute | solution.py:12
  197.7 1.0 gather_fusion.9
  198.8 1.0 gather_fusion.8
  199.8 0.7 gather_fusion.7
  200.6 1.9 fusion.6
  202.5 13.3 %all_gather.28 = f32[1024,128]{0,1:T(8,128)S(1)} all-gather(f32[256,128]{0,1:T(8,128)S(1)} %fusion.6), channel_id=1, replica_groups=mesh['sub'=128,'case'=4] {'case'}, dimensions={0}, use_global_device_ids=true | all-gather | bytes 655360 | tf_op jit(solution)/shard_map/all_gather | solution.py:82
  215.8 7.7 %collective-permute-start.3 = (f32[1024,128]{0,1:T(8,128)S(1)}, f32[1024,128]{0,1:T(8,128)S(1)}, u32[]{:S(2)}, u32[]{:S(2)}) collective-permute-start(f32[1024,128]{0,1:T(8,128)S(1)} %all_gather.28), channel_id=1, source_target_pairs={{0,32},{4,36},{8,40},{12,44},{16,48},{20,52},{24,56},{28,60},{32,0... | collective-permute-start | bytes 1572872 | tf_op jit(solution)/shard_map/ppermute | solution.py:12
  223.5 39.6 %collective-permute-done.3 = f32[1024,128]{0,1:T(8,128)S(1)} collective-permute-done((f32[1024,128]{0,1:T(8,128)S(1)}, f32[1024,128]{0,1:T(8,128)S(1)}, u32[]{:S(2)}, u32[]{:S(2)}) %collective-permute-start.3) | collective-permute-done | bytes 524320 | tf_op jit(solution)/shard_map/ppermute | solution.py:12
  263.6 1.0 gather_fusion.12
  264.7 1.0 gather_fusion.11
  265.7 0.7 gather_fusion.10
  266.6 1.9 fusion.5
  268.5 13.3 %all_gather.29 = f32[1024,128]{0,1:T(8,128)S(1)} all-gather(f32[256,128]{0,1:T(8,128)S(1)} %fusion.5), channel_id=1, replica_groups=mesh['sub'=128,'case'=4] {'case'}, dimensions={0}, use_global_device_ids=true | all-gather | bytes 655360 | tf_op jit(solution)/shard_map/all_gather | solution.py:82
  281.8 11.1 %collective-permute-start.4 = (f32[1024,128]{0,1:T(8,128)S(1)}, f32[1024,128]{0,1:T(8,128)S(1)}, u32[]{:S(2)}, u32[]{:S(2)}) collective-permute-start(f32[1024,128]{0,1:T(8,128)S(1)} %all_gather.29), channel_id=1, source_target_pairs={{0,64},{4,68},{8,72},{12,76},{16,80},{20,84},{24,88},{28,92},{32,9... | collective-permute-start | bytes 1572872 | tf_op jit(solution)/shard_map/ppermute | solution.py:12
  292.9 36.6 %collective-permute-done.4 = f32[1024,128]{0,1:T(8,128)S(1)} collective-permute-done((f32[1024,128]{0,1:T(8,128)S(1)}, f32[1024,128]{0,1:T(8,128)S(1)}, u32[]{:S(2)}, u32[]{:S(2)}) %collective-permute-start.4) | collective-permute-done | bytes 524320 | tf_op jit(solution)/shard_map/ppermute | solution.py:12
  330.0 1.0 gather_fusion.15
  331.0 1.0 gather_fusion.14
  332.1 0.7 gather_fusion.13
  332.9 1.9 fusion.4
  334.8 13.0 %all_gather.30 = f32[1024,128]{0,1:T(8,128)S(1)} all-gather(f32[256,128]{0,1:T(8,128)S(1)} %fusion.4), channel_id=1, replica_groups=mesh['sub'=128,'case'=4] {'case'}, dimensions={0}, use_global_device_ids=true | all-gather | bytes 655360 | tf_op jit(solution)/shard_map/all_gather | solution.py:82
  347.8 2.4 collective-permute-start.5
  350.2 10.2 %collective-permute-done.5 = f32[1024,128]{0,1:T(8,128)S(1)} collective-permute-done((f32[1024,128]{0,1:T(8,128)S(1)}, f32[1024,128]{0,1:T(8,128)S(1)}, u32[]{:S(2)}, u32[]{:S(2)}) %collective-permute-start.5) | collective-permute-done | bytes 524320 | tf_op jit(solution)/shard_map/ppermute | solution.py:12
  361.0 1.0 gather_fusion.18
  362.0 1.0 gather_fusion.17
  363.1 0.7 gather_fusion.16
  363.9 1.9 fusion.3
  365.8 13.4 %all_gather.31 = f32[1024,128]{0,1:T(8,128)S(1)} all-gather(f32[256,128]{0,1:T(8,128)S(1)} %fusion.3), channel_id=1, replica_groups=mesh['sub'=128,'case'=4] {'case'}, dimensions={0}, use_global_device_ids=true | all-gather | bytes 655360 | tf_op jit(solution)/shard_map/all_gather | solution.py:82
  379.3 4.0 collective-permute-start.6
  383.3 0.7 dynamic-slice_bitcast_fusion
  384.0 7.9 %collective-permute-done.6 = f32[1024,128]{0,1:T(8,128)S(1)} collective-permute-done((f32[1024,128]{0,1:T(8,128)S(1)}, f32[1024,128]{0,1:T(8,128)S(1)}, u32[]{:S(2)}, u32[]{:S(2)}) %collective-permute-start.6) | collective-permute-done | bytes 524320 | tf_op jit(solution)/shard_map/ppermute | solution.py:12
  392.3 1.0 gather_fusion.21
  393.4 1.0 gather_fusion.20
  394.4 0.7 gather_fusion.19
  395.3 1.9 fusion.2
  397.2 0.8 copy.123
  (101 shorter events, 5.1 us)
Async XLA Ops:
  7.2 47.5 %copy-start.1 = (s32[1,32]{1,0:T(1,128)S(1)}, s32[1,32]{1,0:T(1,128)}, u32[]{:S(2)}) copy-start(s32[1,32]{1,0:T(1,128)} %param.15) | copy-start | bytes 388
  8.9 36.8 %all-to-all-start = ((f32[1,128,256]{2,0,1:T(1,128)}), f32[1,128,256]{2,0,1:T(1,128)S(1)}, u32[]{:S(2)}, u32[]{:S(2)}) async-start(f32[1,128,256]{2,0,1:T(1,128)} %copy.94), calls=%async_computation | async-start | bytes 262144 | tf_op jit(solution)/shard_map/all_to_all | solution.py:20
  45.7 40.8 %all-to-all-start.1 = ((f32[1,128,1024]{2,0,1:T(1,128)}), f32[1,128,1024]{2,0,1:T(1,128)S(1)}, u32[]{:S(2)}, u32[]{:S(2)}) async-start(f32[1,128,1024]{2,0,1:T(1,128)} %copy.96), calls=%async_computation.1 | async-start | bytes 1048576 | tf_op jit(solution)/shard_map/all_to_all | solution.py:19
  52.9 68.1 %all-gather.3.cloned.1.call-start = ((), (), s32[]{:S(2)}) async-start(), calls=%async_computation.2 | async-start | bytes 2621440 | tf_op jit(solution)/shard_map/all_gather | solution.py:52
  54.8 34.0 %copy-start = (s32[1,32]{1,0:T(1,128)S(1)}, s32[1,32]{1,0:T(1,128)}, u32[]{:S(2)}) copy-start(s32[1,32]{1,0:T(1,128)} %param.14) | copy-start | bytes 388
  122.7 3.8 collective-permute-start
  145.0 12.3 %collective-permute-start.1 = (f32[1024,128]{0,1:T(8,128)S(1)}, f32[1024,128]{0,1:T(8,128)S(1)}, u32[]{:S(2)}, u32[]{:S(2)}) collective-permute-start(f32[1024,128]{0,1:T(8,128)S(1)} %all_gather.26), channel_id=1, source_target_pairs={{0,8},{4,12},{8,0},{12,4},{16,24},{20,28},{24,16},{28,20},{32,40},... | collective-permute-start | bytes 1572872 | tf_op jit(solution)/shard_map/ppermute | solution.py:12
  175.9 21.3 %collective-permute-start.2 = (f32[1024,128]{0,1:T(8,128)S(1)}, f32[1024,128]{0,1:T(8,128)S(1)}, u32[]{:S(2)}, u32[]{:S(2)}) collective-permute-start(f32[1024,128]{0,1:T(8,128)S(1)} %all_gather.27), channel_id=1, source_target_pairs={{0,16},{4,20},{8,24},{12,28},{16,0},{20,4},{24,8},{28,12},{32,48},... | collective-permute-start | bytes 1572872 | tf_op jit(solution)/shard_map/ppermute | solution.py:12
  215.8 47.3 %collective-permute-start.3 = (f32[1024,128]{0,1:T(8,128)S(1)}, f32[1024,128]{0,1:T(8,128)S(1)}, u32[]{:S(2)}, u32[]{:S(2)}) collective-permute-start(f32[1024,128]{0,1:T(8,128)S(1)} %all_gather.28), channel_id=1, source_target_pairs={{0,32},{4,36},{8,40},{12,44},{16,48},{20,52},{24,56},{28,60},{32,0... | collective-permute-start | bytes 1572872 | tf_op jit(solution)/shard_map/ppermute | solution.py:12
  281.8 47.7 %collective-permute-start.4 = (f32[1024,128]{0,1:T(8,128)S(1)}, f32[1024,128]{0,1:T(8,128)S(1)}, u32[]{:S(2)}, u32[]{:S(2)}) collective-permute-start(f32[1024,128]{0,1:T(8,128)S(1)} %all_gather.29), channel_id=1, source_target_pairs={{0,64},{4,68},{8,72},{12,76},{16,80},{20,84},{24,88},{28,92},{32,9... | collective-permute-start | bytes 1572872 | tf_op jit(solution)/shard_map/ppermute | solution.py:12
  347.8 12.7 %collective-permute-start.5 = (f32[1024,128]{0,1:T(8,128)S(1)}, f32[1024,128]{0,1:T(8,128)S(1)}, u32[]{:S(2)}, u32[]{:S(2)}) collective-permute-start(f32[1024,128]{0,1:T(8,128)S(1)} %all_gather.30), channel_id=1, source_target_pairs={{0,128},{4,132},{8,136},{12,140},{16,144},{20,148},{24,152},{28,15... | collective-permute-start | bytes 1572872 | tf_op jit(solution)/shard_map/ppermute | solution.py:12
  379.3 12.6 %collective-permute-start.6 = (f32[1024,128]{0,1:T(8,128)S(1)}, f32[1024,128]{0,1:T(8,128)S(1)}, u32[]{:S(2)}, u32[]{:S(2)}) collective-permute-start(f32[1024,128]{0,1:T(8,128)S(1)} %all_gather.31), channel_id=1, source_target_pairs={{0,256},{4,260},{8,264},{12,268},{16,272},{20,276},{24,280},{28,28... | collective-permute-start | bytes 1572872 | tf_op jit(solution)/shard_map/ppermute | solution.py:12
Sparse Core Ops, SparseCore 0:
  90.9 29.9 all-gather.2
